TPU v7x, 256 devices: a whole 4x4x8 slice. The times are simulated.
256 devices in a mesh: graph: 8 (over z), index: 32 (over x, y, core).
Axes of the slice: x: 4, y: 4, z: 8, core: 2. Of those that a mesh axis runs over, the one named last changes fastest.
Arguments:
- features: bfloat16 [65536, 1024], P(('graph', 'index')), may hold values from -6 to 6
- q_weight: bfloat16 [1024, 1024], replicated, may hold values from -0.1875 to 0.1875
- q_bias: float32 [1024], replicated, may hold values from -3 to 3
- w_self: bfloat16 [1024, 1024], replicated, may hold values from -0.125 to 0.125
- w_neigh: bfloat16 [1024, 1024], replicated, may hold values from -0.125 to 0.125
- z_bias: float32 [1024], replicated, may hold values from -3 to 3
- centroids: bfloat16 [8192, 1024], P('index'), may hold values from -0.1875 to 0.1875
- requests: int32 [256, 32, 16], P(('graph', 'index')), may hold values from 0 to 255, as said below
- slots: int32 [65536, 50], P(('graph', 'index')), may hold values from 0 to 511
- importance: float32 [65536, 50], P(('graph', 'index')), may hold values from 0.1 to 10
- labels: int32 [65536, 1], P(('graph', 'index')), may hold values from 0 to 31; in each aligned block of 256 rows (0 to 255, 256 to 511, ...) at most 16 rows name the same one
Outputs:
- scores: bfloat16 [65536, 256], P(('graph', 'index'))
Inputs may be any that keep to these rules, and one draw needn't show every extreme that they name: `requests`: the 16 rows that a device asks of one device are distinct. `labels`: the rows of one device carry any one label at most 16 times.
All inputs are finite; a program needn't handle non-finite values.
Results may differ from a plain program's by a relative error of at most 0.0051.
Values may be sent and summed in bfloat16 or wider, within the bound.
No kernel may reach another device: no remote copies, remote signals or barrier semaphores. Data moves between devices by JAX's collectives and lax.ppermute only.
A program may use at most 64 MiB of HBM per device.

v0:
```python
import jax
import jax.numpy as jnp
from jax import lax
from jax.sharding import PartitionSpec as P


def place_rows(label_rows, peer_count, owner_slots):
    hits = (label_rows[:, None] == jnp.arange(peer_count, dtype=jnp.int32)[None, :]).astype(
        jnp.int32
    )
    ranks = jnp.sum(hits * (jnp.cumsum(hits, axis=0) - 1), axis=1)
    return label_rows * owner_slots + ranks


def one_hot(index, count):
    return (index[:, None] == jnp.arange(count, dtype=jnp.int32)[None, :]).astype(jnp.bfloat16)


def body(
    features,
    q_weight,
    q_bias,
    w_self,
    w_neigh,
    z_bias,
    centroids,
    requests,
    slots,
    importance,
    labels,
):
    row_count = features.shape[0]
    width = features.shape[1]
    peer_count = lax.axis_size("index")
    owner_slots = max(2 * row_count // peer_count, 2)
    fetch_slots = requests.shape[2]
    slot_count = peer_count * fetch_slots
    cent_count = centroids.shape[0]
    me = lax.axis_index("index")
    own_rows = jnp.where(
        jnp.arange(peer_count, dtype=jnp.int32)[:, None, None] == me,
        requests.astype(jnp.float32),
        0.0,
    )
    all_requests = lax.psum(own_rows, "index")
    wanted = lax.dynamic_index_in_dim(all_requests, me, axis=1, keepdims=False).astype(jnp.int32)
    messages = jax.nn.relu(
        jnp.dot(features, q_weight, preferred_element_type=jnp.float32) + q_bias
    ).astype(jnp.bfloat16)
    weights_norm = importance / jnp.sum(importance, axis=1, keepdims=True)
    slot_ids = jnp.arange(slot_count, dtype=jnp.int32)
    mixing = jnp.sum(
        jnp.where(slots[:, :, None] == slot_ids[None, None, :], weights_norm[:, :, None], 0.0),
        axis=1,
    ).astype(jnp.bfloat16)
    outgoing_msgs = jnp.dot(
        one_hot(wanted.reshape(-1), row_count),
        lax.optimization_barrier(messages),
        preferred_element_type=jnp.float32,
    ).astype(jnp.bfloat16)
    fetched = lax.all_to_all(
        outgoing_msgs.reshape(peer_count, fetch_slots, width),
        "index",
        split_axis=0,
        concat_axis=0,
        tiled=True,
    ).reshape(slot_count, width)
    pooled = jnp.dot(mixing, fetched, preferred_element_type=jnp.float32).astype(jnp.bfloat16)
    hidden = jax.nn.relu(
        jnp.dot(features, w_self, preferred_element_type=jnp.float32)
        + jnp.dot(pooled, w_neigh, preferred_element_type=jnp.float32)
        + z_bias
    )
    normed = (hidden * lax.rsqrt(jnp.mean(hidden * hidden, axis=1, keepdims=True) + 1e-06)).astype(
        jnp.bfloat16
    )
    positions = place_rows(labels[:, 0], peer_count, owner_slots)
    pick = one_hot(positions, peer_count * owner_slots)
    outgoing = lax.dot_general(
        pick, normed, (((0,), (0,)), ((), ())), preferred_element_type=jnp.float32
    ).astype(jnp.bfloat16)
    outgoing = outgoing.reshape(peer_count, owner_slots, width)
    arrived = lax.all_to_all(outgoing, "index", split_axis=0, concat_axis=0, tiled=True)
    flat_rows = arrived.reshape(-1, width)
    raw_scores = lax.dot_general(
        flat_rows, centroids, (((1,), (1,)), ((), ())), preferred_element_type=jnp.float32
    ).astype(jnp.bfloat16)
    returned = lax.all_to_all(
        raw_scores.reshape(peer_count, arrived.shape[1], cent_count),
        "index",
        split_axis=0,
        concat_axis=0,
        tiled=True,
    )
    return jnp.dot(
        pick,
        returned.reshape(peer_count * owner_slots, cent_count),
        preferred_element_type=jnp.float32,
    ).astype(jnp.bfloat16)


def solution(mesh):
    return jax.shard_map(
        body,
        mesh=mesh,
        in_specs=(
            P(("graph", "index"), None),
            P(),
            P(),
            P(),
            P(),
            P(),
            P("index", None),
            P(("graph", "index"), None, None),
            P(("graph", "index"), None),
            P(("graph", "index"), None),
            P(("graph", "index"), None),
        ),
        out_specs=P(("graph", "index"), None),
        check_vma=False,
    )
```

profile of v0, /device:TPU:1, one launch (start us, length us, event | category | flops | bytes accessed | tf_op | source)
XLA Modules:
  0.0 201.9 jit_solution(17790053467064373194)
XLA Ops:
  6.5 0.8 convert_bitcast_fusion
  7.4 0.1 copy.20
  7.5 0.9 broadcast_select_fusion
  8.4 0.0 all-reduce.2.cloned.1.call-update
  8.4 0.7 fusion.12
  9.1 0.6 reduce-window.6
  9.7 0.2 slice_reduce_fusion
  9.9 2.6 %fusion.13 = f32[256,1024]{1,0:T(8,128)S(1)} fusion(bf16[256,1024]{1,0:T(8,128)(2,1)} %param.11, bf16[1024,1024]{1,0:T(8,128)(2,1)} %param.14), kind=kOutput, calls=%fused_computation.37 | convolution fusion | flops 536870912 | bytes 3670016 | tf_op jit(solution)/shard_map/dot_general | solution.py:70
  12.6 0.0 copy-start.3
  12.6 2.6 %fusion.3 = bf16[256,1024]{1,0:T(8,128)(2,1)} fusion(bf16[256,1024]{1,0:T(8,128)(2,1)} %param.11, bf16[1024,1024]{1,0:T(8,128)(2,1)S(1)} %copy-done.4, f32[1024]{0:T(1024)S(1)} %copy-done.6), kind=kOutput, calls=%fused_computation.9 | convolution fusion | flops 537657344 | bytes 3149824 | tf_op jit(solution)/shard_map/dot_general | solution.py:48
  15.1 0.1 fusion.11
  15.2 113.5 %all-reduce.2.cloned.1.call-done = f32[32,32,16]{2,0,1:T(8,128)} async-done(((f32[32,32,16]{2,0,1:T(8,128)}), f32[32,32,16]{2,0,1:T(8,128)}) %all-reduce.2.cloned.1.call-update) | async-done | bytes 65552 | tf_op jit(solution)/shard_map/psum | solution.py:45
  128.7 0.7 dynamic-slice_convert_fusion
  129.4 0.1 convert_element_type.48
  129.5 2.6 %convolution_convert_fusion.1 = bf16[512,1024]{1,0:T(8,128)(2,1)} fusion(bf16[256,1024]{1,0:T(8,128)(2,1)} %fusion.3, s32[512]{0:T(512)S(1)} %convert_element_type.48), kind=kOutput, calls=%fused_computation.3 | convolution fusion | flops 269090816 | bytes 1574912 | tf_op jit(solution)/shard_map/dot_general | solution.py:56
  132.1 6.1 %all-to-all-start = ((bf16[32,16,1024]{2,1,0:T(8,128)(2,1)}), bf16[32,16,1024]{2,1,0:T(8,128)(2,1)}, u32[]{:S(2)}, u32[]{:S(2)}) async-start(bf16[32,16,1024]{2,1,0:T(8,128)(2,1)} %bitcast.6), calls=%async_computation | async-start | bytes 2097152 | tf_op jit(solution)/shard_map/all_to_all | solution.py:61
  138.3 4.3 %select_reduce_fusion = bf16[256,512]{1,0:T(8,128)(2,1)S(1)} fusion(f32[256,50]{0,1:T(8,128)S(1)} %broadcast_divide_fusion, s32[256,50]{0,1:T(8,128)S(1)} %copy-done.2), kind=kLoop, calls=%fused_computation | loop fusion | flops 19529728 | bytes 364544 | tf_op jit(solution)/shard_map/reduce_sum | solution.py:52
  142.6 12.5 %all-to-all-done = bf16[32,16,1024]{2,1,0:T(8,128)(2,1)} async-done(((bf16[32,16,1024]{2,1,0:T(8,128)(2,1)}), bf16[32,16,1024]{2,1,0:T(8,128)(2,1)}, u32[]{:S(2)}, u32[]{:S(2)}) %all-to-all-start) | async-done | bytes 1048608 | tf_op jit(solution)/shard_map/all_to_all | solution.py:61
  155.2 3.3 %multiply_reduce_fusion = (f32[256]{0:T(256)S(1)}, f32[256,1024]{1,0:T(8,128)}) fusion(f32[1024]{0:T(1024)S(1)} %copy-done.7, f32[256,1024]{1,0:T(8,128)S(1)} %fusion.13, bf16[1024,1024]{1,0:T(8,128)(2,1)S(1)} %copy-done, bf16[512,1024]{1,0:T(8,128)(2,1)} %bitcast.7, bf16[256,512]{1,0:T(8,128)(2,1)S(1)} %select_reduce_fusion), kind=kOutput, calls=%fused_computation.14 | convolution fusion | flops 806878976 | bytes 5510144 | tf_op jit(solution)/shard_map/dot_general | solution.py:71
  158.4 1.8 convolution_convert_fusion
  160.3 20.6 %all_to_all.15 = bf16[32,16,1024]{2,1,0:T(8,128)(2,1)S(1)} all-to-all(bf16[32,16,1024]{2,1,0:T(8,128)(2,1)S(1)} %bitcast.40), channel_id=1, replica_groups=mesh['graph'=8,'index'=32] {'index'}, dimensions={0} | all-to-all | bytes 2097152 | tf_op jit(solution)/shard_map/all_to_all | solution.py:83
  180.9 0.5 convolution_convert_fusion.3
  181.4 12.7 %all_to_all.16 = bf16[32,16,256]{2,1,0:T(8,128)(2,1)S(1)} all-to-all(bf16[32,16,256]{2,1,0:T(8,128)(2,1)S(1)} %bitcast.43), channel_id=1, replica_groups=mesh['graph'=8,'index'=32] {'index'}, dimensions={0} | all-to-all | bytes 524288 | tf_op jit(solution)/shard_map/all_to_all | solution.py:88
  194.1 0.9 convolution_convert_fusion.4
  (23 shorter events, 0.1 us)
Async XLA Ops:
  6.5 148.6 %copy-start = (bf16[1024,1024]{1,0:T(8,128)(2,1)S(1)}, bf16[1024,1024]{1,0:T(8,128)(2,1)}, u32[]{:S(2)}) copy-start(bf16[1024,1024]{1,0:T(8,128)(2,1)} %param.15) | copy-start | bytes 6291460
  6.5 122.2 %all-reduce.2.cloned.1.call-start = ((), (), s32[]{:S(2)}) async-start(), calls=%async_computation.3 | async-start | bytes 1048576 | tf_op jit(solution)/shard_map/psum | solution.py:45
  8.4 4.1 %copy-start.6 = (f32[1024]{0:T(1024)S(1)}, f32[1024]{0:T(1024)}, u32[]{:S(2)}) copy-start(f32[1024]{0:T(1024)} %param.13) | copy-start | bytes 12292
  9.9 2.6 %copy-start.4 = (bf16[1024,1024]{1,0:T(8,128)(2,1)S(1)}, bf16[1024,1024]{1,0:T(8,128)(2,1)}, u32[]{:S(2)}) copy-start(bf16[1024,1024]{1,0:T(8,128)(2,1)} %param.12) | copy-start | bytes 6291460
  12.6 2.6 %copy-start.3 = (s32[256,1]{0,1:T(1,128)S(1)}, s32[256,1]{0,1:T(1,128)}, u32[]{:S(2)}) copy-start(s32[256,1]{0,1:T(1,128)} %param.21) | copy-start | bytes 3076
  15.1 123.1 %copy-start.1 = (f32[256,50]{0,1:T(8,128)S(1)}, f32[256,50]{0,1:T(8,128)}, u32[]{:S(2)}) copy-start(f32[256,50]{0,1:T(8,128)} %param.20) | copy-start | bytes 153604
  15.1 123.1 %copy-start.2 = (s32[256,50]{0,1:T(8,128)S(1)}, s32[256,50]{0,1:T(8,128)}, u32[]{:S(2)}) copy-start(s32[256,50]{0,1:T(8,128)} %param.19) | copy-start | bytes 153604
  129.5 25.6 %copy-start.7 = (f32[1024]{0:T(1024)S(1)}, f32[1024]{0:T(1024)}, u32[]{:S(2)}) copy-start(f32[1024]{0:T(1024)} %param.16) | copy-start | bytes 12292
  132.1 23.0 %all-to-all-start = ((bf16[32,16,1024]{2,1,0:T(8,128)(2,1)}), bf16[32,16,1024]{2,1,0:T(8,128)(2,1)}, u32[]{:S(2)}, u32[]{:S(2)}) async-start(bf16[32,16,1024]{2,1,0:T(8,128)(2,1)} %bitcast.6), calls=%async_computation | async-start | bytes 2097152 | tf_op jit(solution)/shard_map/all_to_all | solution.py:61
  158.4 22.5 %copy-start.5 = (bf16[256,1024]{1,0:T(8,128)(2,1)S(1)}, bf16[256,1024]{1,0:T(8,128)(2,1)}, u32[]{:S(2)}) copy-start(bf16[256,1024]{1,0:T(8,128)(2,1)} %param.17) | copy-start | bytes 1572868
Sparse Core Ops, SparseCore 0:
  10.5 118.1 all-reduce.1
where the time goes:
time: 202 us
  waiting for transfers between devices  126 us (62%)
  blocking collectives  33.3 us (16%)
  matrix products  14.3 us (7%)
  between operations  13.5 us (7%)
  other arithmetic  8.31 us (4%)
  starting transfers between devices  6.08 us (3%)
    psum x1, waiting for transfers between devices, body(): all_requests = lax.psum(own_rows, 'index')  113 us
    all_to_all x1, blocking collectives, body(): lax.all_to_all(outgoing, 'index', split_axis=0, concat_axis=0, tiled=True)  20.6 us
    all_to_all x1, blocking collectives, body(): lax.all_to_all(raw_scores.reshape(peer_count, arrived.shape[1], cent_coun...  12.7 us
    all_to_all x1, waiting for transfers between devices, body(): lax.all_to_all(outgoing_msgs.reshape(peer_count, fetch_slots, width), 'in...  12.5 us
    all_to_all x1, starting transfers between devices, body(): lax.all_to_all(outgoing_msgs.reshape(peer_count, fetch_slots, width), 'in...  6.08 us
    reduce_sum x1, other arithmetic, body(): jnp.sum(jnp.where(slots[:, :, None] == slot_ids[None, None, :], weights_n...  4.35 us
  transfers between devices with their start and end apart: 2, of which 2 were waited for; matrix products, arithmetic and copies ran while one was open for 6% of the time, Pallas kernels for 0%

commit v1 on v0

--- a/solution.py
+++ b/solution.py
@@ -42,7 +42,11 @@
         requests.astype(jnp.float32),
         0.0,
     )
-    all_requests = lax.psum(own_rows, "index")
+    all_requests = own_rows
+    for hop in (1, 2, 4, 8, 16):
+        all_requests = all_requests + lax.ppermute(
+            all_requests, "index", [(dev, dev ^ hop) for dev in range(32)]
+        )
     wanted = lax.dynamic_index_in_dim(all_requests, me, axis=1, keepdims=False).astype(jnp.int32)
     messages = jax.nn.relu(
         jnp.dot(features, q_weight, preferred_element_type=jnp.float32) + q_bias

time: 202 us -> 130 us (0.64)
  waiting for transfers between devices: 126 us -> 59.1 us
  between operations: 13.5 us -> 0.2 us
  starting transfers between devices: 6.08 us -> 15 us
    psum x1 -> x0, waiting for transfers between devices: 113 us -> none  [body(): all_requests = lax.psum(own_rows, 'index')]
    ppermute x0 -> x5, waiting for transfers between devices: none -> 46.5 us  [body(): lax.ppermute(all_requests, 'index', [(dev, dev ^ hop) for dev in range(32)])]
    ppermute x0 -> x5, starting transfers between devices: none -> 5.93 us  [body(): lax.ppermute(all_requests, 'index', [(dev, dev ^ hop) for dev in range(32)])]
    all_to_all x1, starting transfers between devices: 6.08 us -> 9.03 us  [body(): lax.all_to_all(outgoing_msgs.reshape(peer_count, fetch_slots, width), 'in...]
  transfers between devices with their start and end apart: 2 -> 6, of which waited for: 2 -> 5; matrix products, arithmetic and copies ran while one was open for 6% -> 8% of each run, Pallas kernels for 0% -> 0%
where the time goes in v1:
time: 130 us
  waiting for transfers between devices  59.1 us (45%)
  blocking collectives  33.3 us (26%)
  starting transfers between devices  15 us (12%)
  matrix products  14.1 us (11%)
  other arithmetic  7.6 us (6%)
    ppermute x5, waiting for transfers between devices, body(): lax.ppermute(all_requests, 'index', [(dev, dev ^ hop) for dev in range(32)])  46.5 us
    all_to_all x1, blocking collectives, body(): lax.all_to_all(outgoing, 'index', split_axis=0, concat_axis=0, tiled=True)  20.6 us
    all_to_all x1, blocking collectives, body(): lax.all_to_all(raw_scores.reshape(peer_count, arrived.shape[1], cent_coun...  12.7 us
    all_to_all x1, waiting for transfers between devices, body(): lax.all_to_all(outgoing_msgs.reshape(peer_count, fetch_slots, width), 'in...  12.5 us
    all_to_all x1, starting transfers between devices, body(): lax.all_to_all(outgoing_msgs.reshape(peer_count, fetch_slots, width), 'in...  9.03 us
    ppermute x5, starting transfers between devices, body(): lax.ppermute(all_requests, 'index', [(dev, dev ^ hop) for dev in range(32)])  5.93 us
    reduce_sum x1, other arithmetic, body(): jnp.sum(jnp.where(slots[:, :, None] == slot_ids[None, None, :], weights_n...  4.35 us
    dot_general x1, matrix products, body(): jnp.dot(features, w_self, preferred_element_type=jnp.float32)  3.47 us
  transfers between devices with their start and end apart: 6, of which 5 were waited for; matrix products, arithmetic and copies ran while one was open for 8% of the time, Pallas kernels for 0%

profile of v1, /device:TPU:1, one launch (start us, length us, event | category | flops | bytes accessed | tf_op | source)
XLA Modules:
  0.0 129.6 jit_solution(8537769343348493927)
XLA Ops:
  0.0 0.8 convert_bitcast_fusion
  1.1 3.3 %collective-permute-start = (f32[32,32,16]{2,0,1:T(8,128)S(1)}, f32[32,32,16]{2,0,1:T(8,128)S(1)}, u32[]{:S(2)}, u32[]{:S(2)}) collective-permute-start(f32[32,32,16]{2,0,1:T(8,128)S(1)} %broadcast_select_fusion), channel_id=1, source_target_pairs={{0,1},{1,0},{2,3},{3,2},{4,5},{5,4},{6,7},{7,6},{8,9},{9,8},{10,11... | collective-permute-start | bytes 196616 | tf_op jit(solution)/shard_map/ppermute | solution.py:47
  4.4 3.5 %fusion.15 = f32[256,1024]{1,0:T(8,128)} fusion(bf16[256,1024]{1,0:T(8,128)(2,1)} %param.11, bf16[1024,1024]{1,0:T(8,128)(2,1)} %param.14), kind=kOutput, calls=%fused_computation.39 | convolution fusion | flops 536870912 | bytes 3670016 | tf_op jit(solution)/shard_map/dot_general | solution.py:74
  8.1 1.5 %fusion.3 = bf16[256,1024]{1,0:T(8,128)(2,1)} fusion(bf16[256,1024]{1,0:T(8,128)(2,1)S(1)} %copy-done.2, bf16[1024,1024]{1,0:T(8,128)(2,1)S(1)} %copy-done.6, f32[1024]{0:T(1024)S(1)} %copy-done.8), kind=kOutput, calls=%fused_computation.9 | convolution fusion | flops 537657344 | bytes 3149824 | tf_op jit(solution)/shard_map/dot_general | solution.py:52
  9.7 11.8 %collective-permute-done.1 = f32[32,32,16]{2,0,1:T(8,128)S(1)} collective-permute-done((f32[32,32,16]{2,0,1:T(8,128)S(1)}, f32[32,32,16]{2,0,1:T(8,128)S(1)}, u32[]{:S(2)}, u32[]{:S(2)}) %collective-permute-start.1) | collective-permute-done | bytes 65568 | tf_op jit(solution)/shard_map/ppermute | solution.py:47
  21.4 0.2 fusion.27
  21.6 1.3 %collective-permute-start.2 = (f32[32,32,16]{2,0,1:T(8,128)S(1)}, f32[32,32,16]{2,0,1:T(8,128)}, u32[]{:S(2)}, u32[]{:S(2)}) collective-permute-start(f32[32,32,16]{2,0,1:T(8,128)S(1)} %fusion.27), channel_id=1, source_target_pairs={{0,4},{1,5},{2,6},{3,7},{4,0},{5,1},{6,2},{7,3},{8,12},{9,13},{10,... | collective-permute-start | bytes 196616 | tf_op jit(solution)/shard_map/ppermute | solution.py:47
  22.9 0.6 reduce-window.6
  23.5 12.3 %collective-permute-done.2 = f32[32,32,16]{2,0,1:T(8,128)} collective-permute-done((f32[32,32,16]{2,0,1:T(8,128)S(1)}, f32[32,32,16]{2,0,1:T(8,128)}, u32[]{:S(2)}, u32[]{:S(2)}) %collective-permute-start.2) | collective-permute-done | bytes 65568 | tf_op jit(solution)/shard_map/ppermute | solution.py:47
  35.8 1.1 add.59
  37.0 0.2 slice_reduce_fusion
  37.2 11.4 %collective-permute-done.3 = f32[32,32,16]{2,0,1:T(8,128)S(1)} collective-permute-done((f32[32,32,16]{2,0,1:T(8,128)S(1)}, f32[32,32,16]{2,0,1:T(8,128)S(1)}, u32[]{:S(2)}, u32[]{:S(2)}) %collective-permute-start.3) | collective-permute-done | bytes 65568 | tf_op jit(solution)/shard_map/ppermute | solution.py:47
  48.7 1.1 collective-permute-start.4
  50.0 11.1 %collective-permute-done.4 = f32[32,32,16]{2,0,1:T(8,128)S(1)} collective-permute-done((f32[32,32,16]{2,0,1:T(8,128)S(1)}, f32[32,32,16]{2,0,1:T(8,128)S(1)}, u32[]{:S(2)}, u32[]{:S(2)}) %collective-permute-start.4) | collective-permute-done | bytes 65568 | tf_op jit(solution)/shard_map/ppermute | solution.py:47
  61.2 2.6 %convolution_convert_fusion.1 = bf16[512,1024]{1,0:T(8,128)(2,1)} fusion(bf16[256,1024]{1,0:T(8,128)(2,1)} %fusion.3, s32[512]{0:T(512)S(1)} %convert_element_type.48), kind=kOutput, calls=%fused_computation.3 | convolution fusion | flops 269090816 | bytes 1574912 | tf_op jit(solution)/shard_map/dot_general | solution.py:60
  63.8 9.0 %all-to-all-start = ((bf16[32,16,1024]{2,1,0:T(8,128)(2,1)}), bf16[32,16,1024]{2,1,0:T(8,128)(2,1)}, u32[]{:S(2)}, u32[]{:S(2)}) async-start(bf16[32,16,1024]{2,1,0:T(8,128)(2,1)} %bitcast.6), calls=%async_computation | async-start | bytes 2097152 | tf_op jit(solution)/shard_map/all_to_all | solution.py:65
  72.9 4.3 %select_reduce_fusion = bf16[256,512]{1,0:T(8,128)(2,1)S(1)} fusion(f32[256,50]{0,1:T(8,128)S(1)} %broadcast_divide_fusion, s32[256,50]{0,1:T(8,128)S(1)} %copy-done.4), kind=kLoop, calls=%fused_computation | loop fusion | flops 19529728 | bytes 364544 | tf_op jit(solution)/shard_map/reduce_sum | solution.py:56
  77.2 12.5 %all-to-all-done = bf16[32,16,1024]{2,1,0:T(8,128)(2,1)} async-done(((bf16[32,16,1024]{2,1,0:T(8,128)(2,1)}), bf16[32,16,1024]{2,1,0:T(8,128)(2,1)}, u32[]{:S(2)}, u32[]{:S(2)}) %all-to-all-start) | async-done | bytes 1048608 | tf_op jit(solution)/shard_map/all_to_all | solution.py:65
  89.8 3.2 %multiply_reduce_fusion = (f32[256]{0:T(256)S(1)}, f32[256,1024]{1,0:T(8,128)}) fusion(f32[1024]{0:T(1024)S(1)} %copy-done.9, f32[256,1024]{1,0:T(8,128)S(1)} %copy-done.1, bf16[1024,1024]{1,0:T(8,128)(2,1)S(1)} %copy-done, bf16[512,1024]{1,0:T(8,128)(2,1)} %bitcast.7, bf16[256,512]{1,0:T(8,128)(2,1)S(1)} %select_reduce_fusion), kind=kOutput, calls=%fused_computation.14 | convolution fusion | flops 806878976 | bytes 5510144 | tf_op jit(solution)/shard_map/dot_general | solution.py:75
  93.0 1.8 %convolution_convert_fusion = bf16[512,1024]{1,0:T(8,128)(2,1)S(1)} fusion(f32[256,1024]{1,0:T(8,128)} %get-tuple-element.6, f32[256]{0:T(256)S(1)} %add_rsqrt_fusion, s32[256]{0:T(256)S(1)} %bitcast.46), kind=kOutput, calls=%fused_computation.2 | convolution fusion | flops 269615104 | bytes 2099200 | tf_op jit(solution)/shard_map/dot_general | solution.py:83
  94.9 20.6 %all_to_all.15 = bf16[32,16,1024]{2,1,0:T(8,128)(2,1)S(1)} all-to-all(bf16[32,16,1024]{2,1,0:T(8,128)(2,1)S(1)} %bitcast.40), channel_id=1, replica_groups=mesh['graph'=8,'index'=32] {'index'}, dimensions={0} | all-to-all | bytes 2097152 | tf_op jit(solution)/shard_map/all_to_all | solution.py:87
  115.5 0.5 convolution_convert_fusion.3
  116.0 12.7 %all_to_all.16 = bf16[32,16,256]{2,1,0:T(8,128)(2,1)S(1)} all-to-all(bf16[32,16,256]{2,1,0:T(8,128)(2,1)S(1)} %bitcast.43), channel_id=1, replica_groups=mesh['graph'=8,'index'=32] {'index'}, dimensions={0} | all-to-all | bytes 524288 | tf_op jit(solution)/shard_map/all_to_all | solution.py:92
  128.7 0.9 convolution_convert_fusion.4
  (38 shorter events, 0.9 us)
Async XLA Ops:
  0.0 89.8 %copy-start = (bf16[1024,1024]{1,0:T(8,128)(2,1)S(1)}, bf16[1024,1024]{1,0:T(8,128)(2,1)}, u32[]{:S(2)}) copy-start(bf16[1024,1024]{1,0:T(8,128)(2,1)} %param.15) | copy-start | bytes 6291460
  1.1 7.0 %copy-start.2 = (bf16[256,1024]{1,0:T(8,128)(2,1)S(1)}, bf16[256,1024]{1,0:T(8,128)(2,1)}, u32[]{:S(2)}) copy-start(bf16[256,1024]{1,0:T(8,128)(2,1)} %param.11) | copy-start | bytes 1572868
  1.1 7.0 %copy-start.6 = (bf16[1024,1024]{1,0:T(8,128)(2,1)S(1)}, bf16[1024,1024]{1,0:T(8,128)(2,1)}, u32[]{:S(2)}) copy-start(bf16[1024,1024]{1,0:T(8,128)(2,1)} %param.12) | copy-start | bytes 6291460
  1.1 7.0 %copy-start.8 = (f32[1024]{0:T(1024)S(1)}, f32[1024]{0:T(1024)}, u32[]{:S(2)}) copy-start(f32[1024]{0:T(1024)} %param.13) | copy-start | bytes 12292
  1.1 6.8 %collective-permute-start = (f32[32,32,16]{2,0,1:T(8,128)S(1)}, f32[32,32,16]{2,0,1:T(8,128)S(1)}, u32[]{:S(2)}, u32[]{:S(2)}) collective-permute-start(f32[32,32,16]{2,0,1:T(8,128)S(1)} %broadcast_select_fusion), channel_id=1, source_target_pairs={{0,1},{1,0},{2,3},{3,2},{4,5},{5,4},{6,7},{7,6},{8,9},{9,8},{10,11... | collective-permute-start | bytes 196616 | tf_op jit(solution)/shard_map/ppermute | solution.py:47
  8.0 14.9 %copy-start.5 = (s32[256,1]{0,1:T(1,128)S(1)}, s32[256,1]{0,1:T(1,128)}, u32[]{:S(2)}) copy-start(s32[256,1]{0,1:T(1,128)} %param.21) | copy-start | bytes 3076
  8.0 13.4 %collective-permute-start.1 = (f32[32,32,16]{2,0,1:T(8,128)S(1)}, f32[32,32,16]{2,0,1:T(8,128)S(1)}, u32[]{:S(2)}, u32[]{:S(2)}) collective-permute-start(f32[32,32,16]{2,0,1:T(8,128)S(1)} %fusion.10), channel_id=1, source_target_pairs={{0,2},{1,3},{2,0},{3,1},{4,6},{5,7},{6,4},{7,5},{8,10},{9,11},{10,... | collective-permute-start | bytes 196616 | tf_op jit(solution)/shard_map/ppermute | solution.py:47
  21.6 14.2 %collective-permute-start.2 = (f32[32,32,16]{2,0,1:T(8,128)S(1)}, f32[32,32,16]{2,0,1:T(8,128)}, u32[]{:S(2)}, u32[]{:S(2)}) collective-permute-start(f32[32,32,16]{2,0,1:T(8,128)S(1)} %fusion.27), channel_id=1, source_target_pairs={{0,4},{1,5},{2,6},{3,7},{4,0},{5,1},{6,2},{7,3},{8,12},{9,13},{10,... | collective-permute-start | bytes 196616 | tf_op jit(solution)/shard_map/ppermute | solution.py:47
  36.9 11.7 %collective-permute-start.3 = (f32[32,32,16]{2,0,1:T(8,128)S(1)}, f32[32,32,16]{2,0,1:T(8,128)S(1)}, u32[]{:S(2)}, u32[]{:S(2)}) collective-permute-start(f32[32,32,16]{2,0,1:T(8,128)S(1)} %add.59), channel_id=1, source_target_pairs={{0,8},{1,9},{2,10},{3,11},{4,12},{5,13},{6,14},{7,15},{8,0},{9,1},... | collective-permute-start | bytes 196616 | tf_op jit(solution)/shard_map/ppermute | solution.py:47
  48.7 24.1 %copy-start.3 = (f32[256,50]{0,1:T(8,128)S(1)}, f32[256,50]{0,1:T(8,128)}, u32[]{:S(2)}) copy-start(f32[256,50]{0,1:T(8,128)} %param.20) | copy-start | bytes 153604
  48.7 24.2 %copy-start.4 = (s32[256,50]{0,1:T(8,128)S(1)}, s32[256,50]{0,1:T(8,128)}, u32[]{:S(2)}) copy-start(s32[256,50]{0,1:T(8,128)} %param.19) | copy-start | bytes 153604
  48.7 12.4 %collective-permute-start.4 = (f32[32,32,16]{2,0,1:T(8,128)S(1)}, f32[32,32,16]{2,0,1:T(8,128)S(1)}, u32[]{:S(2)}, u32[]{:S(2)}) collective-permute-start(f32[32,32,16]{2,0,1:T(8,128)S(1)} %add.60), channel_id=1, source_target_pairs={{0,16},{1,17},{2,18},{3,19},{4,20},{5,21},{6,22},{7,23},{8,24},{9,... | collective-permute-start | bytes 196616 | tf_op jit(solution)/shard_map/ppermute | solution.py:47
  61.2 28.6 %copy-start.1 = (f32[256,1024]{1,0:T(8,128)S(1)}, f32[256,1024]{1,0:T(8,128)}, u32[]{:S(2)}) copy-start(f32[256,1024]{1,0:T(8,128)} %fusion.15) | copy-start | bytes 3145732
  61.2 28.6 %copy-start.9 = (f32[1024]{0:T(1024)S(1)}, f32[1024]{0:T(1024)}, u32[]{:S(2)}) copy-start(f32[1024]{0:T(1024)} %param.16) | copy-start | bytes 12292
  63.8 26.0 %all-to-all-start = ((bf16[32,16,1024]{2,1,0:T(8,128)(2,1)}), bf16[32,16,1024]{2,1,0:T(8,128)(2,1)}, u32[]{:S(2)}, u32[]{:S(2)}) async-start(bf16[32,16,1024]{2,1,0:T(8,128)(2,1)} %bitcast.6), calls=%async_computation | async-start | bytes 2097152 | tf_op jit(solution)/shard_map/all_to_all | solution.py:65
  93.0 22.5 %copy-start.7 = (bf16[256,1024]{1,0:T(8,128)(2,1)S(1)}, bf16[256,1024]{1,0:T(8,128)(2,1)}, u32[]{:S(2)}) copy-start(bf16[256,1024]{1,0:T(8,128)(2,1)} %param.17) | copy-start | bytes 1572868
